TPU v7x, 32 devices: a whole 2x2x4 slice. The times are simulated.
32 devices in a mesh: ind: 8 (over z, x), var: 4 (over y, core).
Axes of the slice: x: 2, y: 2, z: 4, core: 2. Of those that a mesh axis runs over, the one named last changes fastest.
Arguments:
- genotypes: float32 [256, 16384], P('var', 'ind'), may hold values from -30 to 30
- variance_comp: float32 [2], replicated, may hold values from 0.5 to 1.5
- grm_tiles: bfloat16 [80, 512, 512], P('ind'), may hold values from -1 to 6, as said below
- tile_rows: int32 [80], P('ind'), may hold values from 0 to 3, as said below
- tile_cols: int32 [80], P('ind'), may hold values from 0 to 31, as said below
- tile_live: int32 [8], P('ind'), may hold values from 5 to 10, as said below
Outputs:
- solution: float32 [256, 16384], P('var', 'ind')
- gene_gram: float32 [256, 4], P('var')
Inputs may be any that keep to these rules, and one draw needn't show every extreme that they name: `grm_tiles`: every diagonal tile is symmetric, and the tiles of two live slots that form a transposed pair are transposes of each other, so K is symmetric. Slots r < 4 of each index i of ind hold its diagonal tiles: tile_rows = r and tile_cols = i * 4 + r. `tile_cols`: every other slot of index i names a column tile j * 4 + ((i + t) mod 4) of another index j != i, with t < 2. Live off slots come in transposed pairs: a live slot of i at row tile r naming column tile j * 4 + u goes with a live slot of j at row tile u naming column tile i * 4 + r. Some index uses 2 distinct column tiles of one other index. `tile_live`: some index of ind uses all 10 slots.
All inputs are finite; a program needn't handle non-finite values.
Results may differ from a plain program's by a relative error of at most 0.0003.
Values sent between devices are 32-bit elements; how exact they have to be, the bound alone decides.
No kernel may reach another device: no remote copies, remote signals or barrier semaphores. Data moves between devices by JAX's collectives and lax.ppermute only.
A program may use at most 192 MiB of HBM per device.

v0:
```python
import jax
import jax.numpy as jnp
from jax import lax
from jax.sharding import PartitionSpec as P

VARS_GENE = 4
GENES = 64
ITERS = 2
NEED = 2


def local(genotypes, variance_comp, grm_tiles, tile_rows, tile_cols, tile_live):
    cols_here, rows_here = genotypes.shape
    tile_size = grm_tiles.shape[1]
    slot_count = grm_tiles.shape[0]
    row_tiles = rows_here // tile_size
    my_index = lax.axis_index("ind")
    peer_count = lax.axis_size("ind")
    tau_noise = variance_comp[0]
    tau_kin = variance_comp[1]
    live_count = tile_live[0]
    diag_tiles = grm_tiles[:row_tiles]
    off_tiles = grm_tiles[row_tiles:]
    diag_values = jnp.diagonal(diag_tiles, axis1=1, axis2=2).astype(jnp.float32).reshape(rows_here)
    precond = tau_noise + tau_kin * diag_values
    off_rows = tile_rows[row_tiles:]
    off_cols = tile_cols[row_tiles:]
    live_mask = (jnp.arange(row_tiles, slot_count, dtype=jnp.int32) < live_count).astype(
        jnp.float32
    )
    onehot = (off_rows[:, None] == jnp.arange(row_tiles, dtype=jnp.int32)[None, :]).astype(
        jnp.float32
    )
    onehot = onehot * live_mask[:, None]
    solution = jnp.zeros_like(genotypes)
    resid = genotypes
    scaled = resid / precond[None, :]
    direction = scaled
    rz_now = lax.psum(jnp.sum(resid * scaled, axis=1), "ind")
    for rounds in range(ITERS):
        pieces = direction.reshape(cols_here, row_tiles, tile_size)
        table = (
            jnp.arange(peer_count, dtype=jnp.int32)[:, None]
            + jnp.arange(NEED, dtype=jnp.int32)[None, :]
        ) % row_tiles
        outgoing = pieces[:, table]
        arrived = lax.all_to_all(outgoing, "ind", split_axis=1, concat_axis=1, tiled=True)
        flat = arrived.reshape(cols_here, peer_count * NEED, tile_size)
        position = off_cols // row_tiles * NEED + (off_cols % row_tiles - my_index) % row_tiles
        position = jnp.clip(position, 0, peer_count * NEED - 1)
        picked = jnp.take(flat, position, axis=1)
        apply_pieces = direction.reshape(cols_here, row_tiles, tile_size)
        near = jnp.einsum(
            "crk,rqk->crq",
            apply_pieces,
            diag_tiles,
            precision=lax.Precision.HIGHEST,
            preferred_element_type=jnp.float32,
        )
        far = jnp.einsum(
            "csk,sqk->csq",
            picked,
            off_tiles,
            precision=lax.Precision.HIGHEST,
            preferred_element_type=jnp.float32,
        )
        far = jnp.einsum("csq,sr->crq", far, onehot, precision=lax.Precision.HIGHEST)
        image = tau_noise * direction + tau_kin * (near + far).reshape(cols_here, rows_here)
        alpha = rz_now / lax.psum(jnp.sum(direction * image, axis=1), "ind")
        solution = solution + alpha[:, None] * direction
        resid = resid - alpha[:, None] * image
        if rounds + 1 < ITERS:
            scaled = resid / precond[None, :]
            rz_next = lax.psum(jnp.sum(resid * scaled, axis=1), "ind")
            direction = scaled + (rz_next / rz_now)[:, None] * direction
            rz_now = rz_next
    var_index = lax.axis_index("var")
    gathered = lax.all_gather(solution, "var", axis=0, tiled=True)
    split_cols = gathered.reshape(VARS_GENE, GENES, rows_here)
    first_gene = var_index * cols_here % GENES
    matching = lax.dynamic_slice_in_dim(split_cols, first_gene, cols_here, 1)
    partial_gram = jnp.einsum("jn,bjn->jb", genotypes, matching, precision=lax.Precision.HIGHEST)
    total_gram = lax.psum(partial_gram, "ind")
    gene_gram = total_gram / (peer_count * rows_here)
    return (solution, gene_gram)


def solution(mesh):
    placed = (P("var", "ind"), P(), P("ind", None, None), P("ind"), P("ind"), P("ind"))
    return jax.shard_map(
        local,
        mesh=mesh,
        in_specs=placed,
        out_specs=(P("var", "ind"), P("var", None)),
        check_vma=False,
    )
```

profile of v0, /device:TPU:0, one launch (start us, length us, event | category | flops | bytes accessed | tf_op | source)
XLA Modules:
  0.0 310.4 jit_solution(10890623376764823809)
XLA Ops:
  7.2 1.6 slice-done
  8.8 41.5 %copy.31 = bf16[4,512,512]{0,2,1:T(8,128)(2,1)} copy(bf16[4,512,512]{2,1,0:T(8,128)(2,1)S(1)} %slice-done) | data formatting | bytes 4194304 | tf_op jit(solution)/shard_map/slice | solution.py:22
  50.9 6.5 %gather_fusion = bf16[512,4]{1,0:T(8,128)(2,1)S(1)} fusion(bf16[4,512,512]{0,2,1:T(8,128)(2,1)} %copy.31, s32[512]{0:T(512)S(1)} %bitcast.54), kind=kCustom, calls=%fused_computation.2 | custom fusion | bytes 12288 | tf_op jit(solution)/shard_map/jit(diagonal)/gather | solution.py:24
  57.4 1.3 multiply_add_fusion.3
  59.0 2.0 gather_fusion.1
  61.1 7.4 %all-to-all-start = ((f32[64,8,2,512]{3,0,2,1:T(8,128)}), f32[64,8,2,512]{3,0,2,1:T(8,128)S(1)}, u32[]{:S(2)}, u32[]{:S(2)}) async-start(f32[64,8,2,512]{3,0,2,1:T(8,128)} %bitcast.60), calls=%async_computation | async-start | bytes 4194304 | tf_op jit(solution)/shard_map/all_to_all | solution.py:47
  69.4 47.3 %all-to-all-done = f32[64,8,2,512]{3,0,2,1:T(8,128)S(1)} async-done(((f32[64,8,2,512]{3,0,2,1:T(8,128)}), f32[64,8,2,512]{3,0,2,1:T(8,128)S(1)}, u32[]{:S(2)}, u32[]{:S(2)}) %all-to-all-start) | async-done | bytes 2097184 | tf_op jit(solution)/shard_map/all_to_all | solution.py:47
  116.7 1.5 gather_fusion.3
  118.2 5.1 %fusion.6 = f32[64,6,512]{2,0,1:T(8,128)S(1)} fusion(bf16[10,512,512]{2,1,0:T(8,128)(2,1)} %param.10, f32[6,64,512]{2,1,0:T(8,128)} %gather_fusion.3, pred[6]{0:T(512)(128)(4,1)S(1)} %get-tuple-element.7), kind=kOutput, calls=%fused_computation.11 | convolution fusion | flops 1208156160 | bytes 4718598 | tf_op jit(solution)/shard_map/csk,sqk->csq/dot_general | solution.py:60
  123.3 1.4 fusion.18
  124.7 4.3 %fusion.15 = f32[4,8,8,512]{3,2,1,0:T(8,128)S(1)} fusion(f32[4,64,512]{2,0,1:T(4,128)S(1)} %fusion.18, f32[]{:T(128)} %bitcast.1, f32[8,4,8,512]{3,2,1,0:T(8,128)S(1)} %bitcast.68, bf16[10,512,512]{2,1,0:T(8,128)(2,1)} %param.10), kind=kOutput, calls=%fused_computation.18 | convolution fusion | flops 805568512 | bytes 3670528 | tf_op jit(solution)/shard_map/crk,rqk->crq/dot_general | solution.py:53
  129.9 19.5 %all-reduce = (f32[64]{0:T(128)S(1)}, f32[64]{0:T(128)S(1)}) all-reduce(f32[64]{0:T(128)S(1)} %get-tuple-element.4, f32[64]{0:T(128)S(1)} %get-tuple-element.3), channel_id=1, replica_groups=mesh['ind'=8,'var'=4] {'ind'}, use_global_device_ids=true, to_apply=%region_1.2 | all-reduce | flops 128 | bytes 1024 | tf_op jit(solution)/shard_map/psum | solution.py:39
  149.4 0.9 multiply_reduce_fusion.1
  150.3 17.1 %psum.37 = f32[64]{0:T(128)S(1)} all-reduce(f32[64]{0:T(128)S(1)} %multiply_reduce_fusion.1), channel_id=1, replica_groups=mesh['ind'=8,'var'=4] {'ind'}, use_global_device_ids=true, to_apply=%region_5.7 | all-reduce | flops 64 | bytes 512 | tf_op jit(solution)/shard_map/psum | solution.py:74
  168.4 2.0 gather_fusion.2
  170.4 45.8 %all_to_all.10 = f32[64,8,2,512]{3,0,2,1:T(8,128)} all-to-all(f32[64,8,2,512]{3,0,2,1:T(8,128)} %bitcast.61), channel_id=1, replica_groups=mesh['ind'=8,'var'=4] {'ind'}, dimensions={1} | all-to-all | bytes 4194304 | tf_op jit(solution)/shard_map/all_to_all | solution.py:47
  216.2 2.2 gather_fusion.4
  218.4 4.9 %fusion.9 = f32[64,6,512]{2,0,1:T(8,128)S(1)} fusion(bf16[10,512,512]{2,1,0:T(8,128)(2,1)} %param.10, f32[6,64,512]{2,1,0:T(8,128)S(1)} %gather_fusion.4, pred[6]{0:T(512)(128)(4,1)S(1)} %get-tuple-element.7), kind=kOutput, calls=%fused_computation.12 | convolution fusion | flops 1208156160 | bytes 4718598 | tf_op jit(solution)/shard_map/csk,sqk->csq/dot_general | solution.py:60
  223.3 1.4 fusion.16
  224.7 4.3 %fusion.13 = f32[4,8,8,512]{3,2,1,0:T(8,128)S(1)} fusion(f32[4,64,512]{2,0,1:T(4,128)S(1)} %fusion.16, f32[]{:T(128)} %bitcast.1, f32[8,4,8,512]{3,2,1,0:T(8,128)S(1)} %bitcast.57, bf16[10,512,512]{2,1,0:T(8,128)(2,1)} %param.10), kind=kOutput, calls=%fused_computation.15 | convolution fusion | flops 805568512 | bytes 3670528 | tf_op jit(solution)/shard_map/crk,rqk->crq/dot_general | solution.py:53
  229.8 19.4 %psum.38 = f32[64]{0:T(128)S(1)} all-reduce(f32[64]{0:T(128)S(1)} %multiply_reduce_fusion), channel_id=1, replica_groups=mesh['ind'=8,'var'=4] {'ind'}, use_global_device_ids=true, to_apply=%region_7.9 | all-reduce | flops 64 | bytes 512 | tf_op jit(solution)/shard_map/psum | solution.py:69
  250.2 20.1 %all-gather.2.cloned.1.call-done = f32[256,2048]{1,0:T(8,128)} async-done(((f32[64,2048]{1,0:T(8,128)}), f32[256,2048]{1,0:T(8,128)}) %all-gather.2.cloned.1.call-update) | async-done | bytes 2097168 | tf_op jit(solution)/shard_map/all_gather | solution.py:78
  270.3 11.3 %fusion.4 = f32[64,1,4]{2,1,0:T(1,128)S(1)} fusion(f32[4,64,2048]{2,1,0:T(8,128)} %bitcast.77, f32[64,2048,1]{1,0,2:T(8,128)S(1)} %bitcast.55), kind=kOutput, calls=%fused_computation.9 | convolution fusion | flops 6291456 | bytes 2622464 | tf_op jit(solution)/shard_map/jn,bjn->jb/dot_general | solution.py:82
  281.6 21.4 %psum.39 = f32[64,4]{0,1:T(4,128)S(1)} all-reduce(f32[64,4]{0,1:T(4,128)S(1)} %bitcast.76), channel_id=1, replica_groups=mesh['ind'=8,'var'=4] {'ind'}, use_global_device_ids=true, to_apply=%region_8.10 | all-reduce | flops 256 | bytes 2048 | tf_op jit(solution)/shard_map/psum | solution.py:83
  (36 shorter events, 5.4 us)
Async XLA Ops:
  7.2 1.6 slice-start
  8.8 41.5 %copy-start.1 = (f32[2]{0:T(128)S(1)}, f32[2]{0:T(128)}, u32[]{:S(2)}) copy-start(f32[2]{0:T(128)} %param.9) | copy-start | bytes 28
  8.8 50.0 %copy-start = (f32[64,2048]{1,0:T(8,128)S(1)}, f32[64,2048]{1,0:T(8,128)}, u32[]{:S(2)}) copy-start(f32[64,2048]{1,0:T(8,128)} %param.8) | copy-start | bytes 1572868
  61.1 8.1 %copy-start.3 = (s32[10]{0:T(128)S(1)}, s32[10]{0:T(128)}, u32[]{:S(2)}) copy-start(s32[10]{0:T(128)} %param.11) | copy-start | bytes 124
  61.1 8.2 %copy-start.2 = (s32[10]{0:T(128)S(1)}, s32[10]{0:T(128)}, u32[]{:S(2)}) copy-start(s32[10]{0:T(128)} %param.12) | copy-start | bytes 124
  61.1 55.7 %all-to-all-start = ((f32[64,8,2,512]{3,0,2,1:T(8,128)}), f32[64,8,2,512]{3,0,2,1:T(8,128)S(1)}, u32[]{:S(2)}, u32[]{:S(2)}) async-start(f32[64,8,2,512]{3,0,2,1:T(8,128)} %bitcast.60), calls=%async_computation | async-start | bytes 4194304 | tf_op jit(solution)/shard_map/all_to_all | solution.py:47
  68.5 201.8 %all-gather.2.cloned.1.call-start = ((), (), s32[]{:S(2)}) async-start(), calls=%async_computation.2 | async-start | bytes 2621440 | tf_op jit(solution)/shard_map/all_gather | solution.py:78
Sparse Core Ops, SparseCore 0:
  250.3 19.8 all-gather.1
where the time goes:
time: 311 us; the launch traced here: 310 us
  blocking collectives  123 us (40%)
  waiting for transfers between devices  67.4 us (22%)
  local copies, waits for them, and re-layouts  58.4 us (19%)
  matrix products  32.6 us (10%)
  between operations  14.8 us (5%)
  starting transfers between devices  7.45 us (2%)
  other arithmetic  6.54 us (2%)
    all_to_all x1, waiting for transfers between devices, local(): lax.all_to_all(outgoing, 'ind', split_axis=1, concat_axis=1, tiled=True)  47.3 us
    all_to_all x1, blocking collectives, local(): lax.all_to_all(outgoing, 'ind', split_axis=1, concat_axis=1, tiled=True)  45.8 us
    slice x3, local copies, waits for them, and re-layouts, local(): diag_tiles = grm_tiles[:row_tiles]  43.1 us
    psum x1, blocking collectives, local(): total_gram = lax.psum(partial_gram, 'ind')  21.4 us
    all_gather x1, waiting for transfers between devices, local(): gathered = lax.all_gather(solution, 'var', axis=0, tiled=True)  20.1 us
    psum x1, blocking collectives, local(): rz_now = lax.psum(jnp.sum(resid * scaled, axis=1), 'ind')  19.5 us
    psum x1, blocking collectives, local(): alpha = rz_now / lax.psum(jnp.sum(direction * image, axis=1), 'ind')  19.4 us
    psum x1, blocking collectives, local(): rz_next = lax.psum(jnp.sum(resid * scaled, axis=1), 'ind')  17.1 us
  transfers between devices with their start and end apart: 2, of which 2 were waited for; matrix products, arithmetic and copies ran while one was open for 0% of the time, Pallas kernels for 0%

commit v1 on v0

--- a/solution.py
+++ b/solution.py
@@ -7,6 +7,24 @@
 GENES = 64
 ITERS = 2
 NEED = 2
+
+
+def laid_out(blocks, dim):
+    blocks = jnp.moveaxis(blocks, 0, dim)
+    shape = blocks.shape
+    return blocks.reshape(*shape[:dim], shape[dim] * shape[dim + 1], *shape[dim + 2 :])
+
+
+def collected_by_bits(x, axis):
+    size = lax.axis_size(axis)
+    parts = x[None]
+    for level in range(size.bit_length() - 1):
+        bit = 1 << level
+        other = lax.ppermute(parts, axis, [(i, i ^ bit) for i in range(size)])
+        both = jnp.stack([parts, other])
+        upper = lax.axis_index(axis) >> level & 1
+        parts = jnp.where(upper == 0, both, both[::-1]).reshape(-1, *x.shape)
+    return parts
 
 
 def local(genotypes, variance_comp, grm_tiles, tile_rows, tile_cols, tile_live):
@@ -75,7 +93,7 @@
             direction = scaled + (rz_next / rz_now)[:, None] * direction
             rz_now = rz_next
     var_index = lax.axis_index("var")
-    gathered = lax.all_gather(solution, "var", axis=0, tiled=True)
+    gathered = laid_out(collected_by_bits(solution, "var"), 0)
     split_cols = gathered.reshape(VARS_GENE, GENES, rows_here)
     first_gene = var_index * cols_here % GENES
     matching = lax.dynamic_slice_in_dim(split_cols, first_gene, cols_here, 1)

time: 311 us -> 300 us (0.965)
  between operations: 14.8 us -> 1.48 us
  waiting for transfers between devices: 67.4 us -> 73.1 us
  blocking collectives: 123 us -> 119 us
    ppermute x0 -> x2, waiting for transfers between devices: none -> 25.7 us  [collected_by_bits(): other = lax.ppermute(parts, axis, [(i, i ^ bit) for i in range(size)])]
    all_gather x1 -> x0, waiting for transfers between devices: 20.1 us -> none  [local(): gathered = lax.all_gather(solution, 'var', axis=0, tiled=True)]
    psum x1, blocking collectives: 21.4 us -> 17.1 us  [local(): total_gram = lax.psum(partial_gram, 'ind')]
  transfers between devices with their start and end apart: 2 -> 3, of which waited for: 2 -> 3; matrix products, arithmetic and copies ran while one was open for 0% -> 0% of each run, Pallas kernels for 0% -> 0%
where the time goes in v1:
time: 300 us
  blocking collectives  119 us (40%)
  waiting for transfers between devices  73.1 us (24%)
  local copies, waits for them, and re-layouts  58.4 us (19%)
  matrix products  31 us (10%)
  starting transfers between devices  9.06 us (3%)
  other arithmetic  7.43 us (2%)
    all_to_all x1, waiting for transfers between devices, local(): lax.all_to_all(outgoing, 'ind', split_axis=1, concat_axis=1, tiled=True)  47.4 us
    all_to_all x1, blocking collectives, local(): lax.all_to_all(outgoing, 'ind', split_axis=1, concat_axis=1, tiled=True)  45.8 us
    slice x3, local copies, waits for them, and re-layouts, local(): diag_tiles = grm_tiles[:row_tiles]  43.1 us
    ppermute x2, waiting for transfers between devices, collected_by_bits(): other = lax.ppermute(parts, axis, [(i, i ^ bit) for i in range(size)])  25.7 us
    psum x1, blocking collectives, local(): alpha = rz_now / lax.psum(jnp.sum(direction * image, axis=1), 'ind')  19.6 us
    psum x1, blocking collectives, local(): rz_now = lax.psum(jnp.sum(resid * scaled, axis=1), 'ind')  19.5 us
    psum x1, blocking collectives, local(): total_gram = lax.psum(partial_gram, 'ind')  17.1 us
    psum x1, blocking collectives, local(): rz_next = lax.psum(jnp.sum(resid * scaled, axis=1), 'ind')  17.1 us
  transfers between devices with their start and end apart: 3, of which 3 were waited for; matrix products, arithmetic and copies ran while one was open for 0% of the time, Pallas kernels for 0%

profile of v1, /device:TPU:0, one launch (start us, length us, event | category | flops | bytes accessed | tf_op | source)
XLA Modules:
  0.0 299.7 jit_solution(7843961947087999338)
XLA Ops:
  0.7 1.6 slice-done
  2.3 41.5 %copy.31 = bf16[4,512,512]{0,2,1:T(8,128)(2,1)} copy(bf16[4,512,512]{2,1,0:T(8,128)(2,1)S(1)} %slice-done) | data formatting | bytes 4194304 | tf_op jit(solution)/shard_map/slice | solution.py:40
  44.4 6.5 %gather_fusion = bf16[512,4]{1,0:T(8,128)(2,1)S(1)} fusion(bf16[4,512,512]{0,2,1:T(8,128)(2,1)} %copy.31, s32[512]{0:T(512)S(1)} %bitcast.62), kind=kCustom, calls=%fused_computation.2 | custom fusion | bytes 12288 | tf_op jit(solution)/shard_map/jit(diagonal)/gather | solution.py:42
  52.5 2.0 gather_fusion.1
  54.5 7.4 %all-to-all-start = ((f32[64,8,2,512]{3,0,2,1:T(8,128)}), f32[64,8,2,512]{3,0,2,1:T(8,128)S(1)}, u32[]{:S(2)}, u32[]{:S(2)}) async-start(f32[64,8,2,512]{3,0,2,1:T(8,128)} %bitcast.68), calls=%async_computation | async-start | bytes 4194304 | tf_op jit(solution)/shard_map/all_to_all | solution.py:65
  62.8 47.4 %all-to-all-done = f32[64,8,2,512]{3,0,2,1:T(8,128)S(1)} async-done(((f32[64,8,2,512]{3,0,2,1:T(8,128)}), f32[64,8,2,512]{3,0,2,1:T(8,128)S(1)}, u32[]{:S(2)}, u32[]{:S(2)}) %all-to-all-start) | async-done | bytes 2097184 | tf_op jit(solution)/shard_map/all_to_all | solution.py:65
  110.2 1.5 gather_fusion.3
  111.6 5.1 %fusion.6 = f32[64,6,512]{2,0,1:T(8,128)S(1)} fusion(bf16[10,512,512]{2,1,0:T(8,128)(2,1)} %param.10, f32[6,64,512]{2,1,0:T(8,128)} %gather_fusion.3, pred[6]{0:T(512)(128)(4,1)S(1)} %get-tuple-element.7), kind=kOutput, calls=%fused_computation.14 | convolution fusion | flops 1208156160 | bytes 4718598 | tf_op jit(solution)/shard_map/csk,sqk->csq/dot_general | solution.py:78
  116.8 1.4 fusion.18
  118.2 4.3 %fusion.15 = f32[4,8,8,512]{3,2,1,0:T(8,128)S(1)} fusion(f32[4,64,512]{2,0,1:T(4,128)S(1)} %fusion.18, f32[]{:T(128)} %bitcast.1, f32[8,4,8,512]{3,2,1,0:T(8,128)S(1)} %bitcast.76, bf16[10,512,512]{2,1,0:T(8,128)(2,1)} %param.10), kind=kOutput, calls=%fused_computation.21 | convolution fusion | flops 805568512 | bytes 3670528 | tf_op jit(solution)/shard_map/crk,rqk->crq/dot_general | solution.py:71
  123.4 19.5 %all-reduce = (f32[64]{0:T(128)S(1)}, f32[64]{0:T(128)S(1)}) all-reduce(f32[64]{0:T(128)S(1)} %get-tuple-element.4, f32[64]{0:T(128)S(1)} %get-tuple-element.3), channel_id=1, replica_groups=mesh['ind'=8,'var'=4] {'ind'}, use_global_device_ids=true, to_apply=%region_1.2 | all-reduce | flops 128 | bytes 1024 | tf_op jit(solution)/shard_map/psum | solution.py:57
  143.8 17.1 %psum.37 = f32[64]{0:T(128)S(1)} all-reduce(f32[64]{0:T(128)S(1)} %multiply_reduce_fusion.1), channel_id=1, replica_groups=mesh['ind'=8,'var'=4] {'ind'}, use_global_device_ids=true, to_apply=%region_5.7 | all-reduce | flops 64 | bytes 512 | tf_op jit(solution)/shard_map/psum | solution.py:92
  161.8 2.0 gather_fusion.2
  163.9 45.8 %all_to_all.10 = f32[64,8,2,512]{3,0,2,1:T(8,128)} all-to-all(f32[64,8,2,512]{3,0,2,1:T(8,128)} %bitcast.69), channel_id=1, replica_groups=mesh['ind'=8,'var'=4] {'ind'}, dimensions={1} | all-to-all | bytes 4194304 | tf_op jit(solution)/shard_map/all_to_all | solution.py:65
  209.7 2.2 gather_fusion.4
  211.9 4.9 %fusion.9 = f32[64,6,512]{2,0,1:T(8,128)S(1)} fusion(bf16[10,512,512]{2,1,0:T(8,128)(2,1)} %param.10, f32[6,64,512]{2,1,0:T(8,128)S(1)} %gather_fusion.4, pred[6]{0:T(512)(128)(4,1)S(1)} %get-tuple-element.7), kind=kOutput, calls=%fused_computation.15 | convolution fusion | flops 1208156160 | bytes 4718598 | tf_op jit(solution)/shard_map/csk,sqk->csq/dot_general | solution.py:78
  216.7 1.4 fusion.16
  218.2 4.3 %fusion.13 = f32[4,8,8,512]{3,2,1,0:T(8,128)S(1)} fusion(f32[4,64,512]{2,0,1:T(4,128)S(1)} %fusion.16, f32[]{:T(128)} %bitcast.1, f32[8,4,8,512]{3,2,1,0:T(8,128)S(1)} %bitcast.65, bf16[10,512,512]{2,1,0:T(8,128)(2,1)} %param.10), kind=kOutput, calls=%fused_computation.18 | convolution fusion | flops 805568512 | bytes 3670528 | tf_op jit(solution)/shard_map/crk,rqk->crq/dot_general | solution.py:71
  223.3 19.6 %psum.38 = f32[64]{0:T(128)S(1)} all-reduce(f32[64]{0:T(128)S(1)} %multiply_reduce_fusion), channel_id=1, replica_groups=mesh['ind'=8,'var'=4] {'ind'}, use_global_device_ids=true, to_apply=%region_7.9 | all-reduce | flops 64 | bytes 512 | tf_op jit(solution)/shard_map/psum | solution.py:87
  243.2 1.9 collective-permute-done
  246.4 1.6 collective-permute-start.1
  248.0 23.8 %collective-permute-done.1 = f32[2,64,2048]{2,1,0:T(8,128)S(1)} collective-permute-done((f32[2,64,2048]{2,1,0:T(8,128)}, f32[2,64,2048]{2,1,0:T(8,128)S(1)}, u32[]{:S(2)}, u32[]{:S(2)}) %collective-permute-start.1) | collective-permute-done | bytes 1048608 | tf_op jit(solution)/shard_map/ppermute | solution.py:23
  272.2 9.7 %fusion.4 = f32[64,1,4]{2,1,0:T(1,128)S(1)} fusion(f32[4,64,2048]{2,1,0:T(8,128)S(1)} %bitcast.78, f32[64,2048,1]{1,0,2:T(8,128)S(1)} %bitcast.63), kind=kOutput, calls=%fused_computation.11 | convolution fusion | flops 6291456 | bytes 2622464 | tf_op jit(solution)/shard_map/jn,bjn->jb/dot_general | solution.py:100
  282.0 17.1 %psum.39 = f32[64,4]{0,1:T(4,128)S(1)} all-reduce(f32[64,4]{0,1:T(4,128)S(1)} %bitcast.89), channel_id=1, replica_groups=mesh['ind'=8,'var'=4] {'ind'}, use_global_device_ids=true, to_apply=%region_8.10 | all-reduce | flops 256 | bytes 2048 | tf_op jit(solution)/shard_map/psum | solution.py:101
  (43 shorter events, 8.6 us)
Async XLA Ops:
  0.7 1.6 slice-start
  2.2 41.5 %copy-start.2 = (f32[2]{0:T(128)S(1)}, f32[2]{0:T(128)}, u32[]{:S(2)}) copy-start(f32[2]{0:T(128)} %param.9) | copy-start | bytes 28
  2.3 50.0 %copy-start = (f32[64,2048]{1,0:T(8,128)S(1)}, f32[64,2048]{1,0:T(8,128)}, u32[]{:S(2)}) copy-start(f32[64,2048]{1,0:T(8,128)} %param.8) | copy-start | bytes 1572868
  54.5 8.1 %copy-start.4 = (s32[10]{0:T(128)S(1)}, s32[10]{0:T(128)}, u32[]{:S(2)}) copy-start(s32[10]{0:T(128)} %param.11) | copy-start | bytes 124
  54.5 8.2 %copy-start.3 = (s32[10]{0:T(128)S(1)}, s32[10]{0:T(128)}, u32[]{:S(2)}) copy-start(s32[10]{0:T(128)} %param.12) | copy-start | bytes 124
  54.5 55.7 %all-to-all-start = ((f32[64,8,2,512]{3,0,2,1:T(8,128)}), f32[64,8,2,512]{3,0,2,1:T(8,128)S(1)}, u32[]{:S(2)}, u32[]{:S(2)}) async-start(f32[64,8,2,512]{3,0,2,1:T(8,128)} %bitcast.68), calls=%async_computation | async-start | bytes 4194304 | tf_op jit(solution)/shard_map/all_to_all | solution.py:65
  243.1 3.3 %copy-start.1 = (f32[64,2048]{1,0:T(8,128)}, f32[64,2048]{1,0:T(8,128)S(1)}, u32[]{:S(2)}) copy-start(f32[64,2048]{1,0:T(8,128)S(1)} %multiply_add_fusion) | copy-start | bytes 1572868
  243.1 2.0 collective-permute-start
  246.4 25.4 %collective-permute-start.1 = (f32[2,64,2048]{2,1,0:T(8,128)}, f32[2,64,2048]{2,1,0:T(8,128)S(1)}, u32[]{:S(2)}, u32[]{:S(2)}) collective-permute-start(f32[2,64,2048]{2,1,0:T(8,128)} %get-tuple-element.10), channel_id=1, source_target_pairs={{0,2},{1,3},{2,0},{3,1},{4,6},{5,7},{6,4},{7,5},{8,10},{9,11},{10,... | collective-permute-start | bytes 3145736 | tf_op jit(solution)/shard_map/ppermute | solution.py:23
